TPU v7x, 256 devices: a whole 4x4x8 slice. The times are simulated.
256 devices in a mesh: dp: 32 (over z_lo, y, x), tensor: 8 (over z_hi, core).
Axes of the slice: x: 4, y: 4, z: 8 (z_hi: 4, z_lo: 2; z = z_hi * 2 + z_lo), core: 2. Of those that a mesh axis runs over, the one named last changes fastest.
Arguments:
- embeds: bfloat16 [512, 4608], P('dp'), may hold values from -6 to 6
- owner: int32 [64, 8], P('dp'), may hold values from 0 to 7, each once within a row
- pairs: int32 [64, 56, 2], P('dp'), may hold values from 0 to 7, as said below
- pref_weight: bfloat16 [2, 4608, 4608], P(None, 'dp', 'tensor'), may hold values from -0.0625 to 0.0625
- pref_bias: float32 [4608], P('tensor'), may hold values from -3 to 3
- pref_out: float32 [4608], P('tensor'), may hold values from -0.375 to 0.375
- logratio: float32 [512], P('dp'), may hold values from -3 to 3
- attn_out: bfloat16 [32768, 4096], P('dp', 'tensor'), may hold values from -6 to 6
- grad_out: bfloat16 [32768, 4608], P('dp', 'tensor'), may hold values from -6 to 6
- w_out: bfloat16 [4608, 4096], P('dp', 'tensor'), may hold values from -0.09375 to 0.09375
Outputs:
- d_attn: bfloat16 [32768, 4096], P('dp', 'tensor')
- o_grad: float32 [4608, 4096], P('dp', 'tensor')
Inputs may be any that keep to these rules, and one draw needn't show every extreme that they name: `pairs`: the two numbers of a pair differ. Each row of owner names every number once.
All inputs are finite; a program needn't handle non-finite values.
Results may differ from a plain program's by a relative error of at most 0.0049.
Values may be sent and summed in bfloat16 or wider, within the bound.
No kernel may reach another device: no remote copies, remote signals or barrier semaphores. Data moves between devices by JAX's collectives and lax.ppermute only.
A program may use at most 128 MiB of HBM per device.

v0:
```python
import jax
import jax.numpy as jnp
from jax import lax
from jax.sharding import PartitionSpec as P

eta_scale = 2.0


def shards(
    embeds, owner, pairs, pref_weight, pref_bias, pref_out, logratio, attn_out, grad_out, w_out
):
    resp_dev = embeds.shape[0]
    prompts_dev = owner.shape[0]
    groups = owner.shape[1]
    npairs = pairs.shape[1]
    width_local = pref_weight.shape[2]
    features = lax.all_gather(grad_out, "tensor", axis=1, tiled=True)
    base = (jnp.arange(prompts_dev, dtype=jnp.int32) * groups)[:, None]
    row_a = base + jnp.take_along_axis(owner, pairs[:, :, 0], axis=1)
    row_b = base + jnp.take_along_axis(owner, pairs[:, :, 1], axis=1)
    left = embeds[row_a.reshape(-1)]
    right = embeds[row_b.reshape(-1)]
    piece = lax.all_gather(pref_weight, "dp", axis=1, tiled=True)
    upper = jnp.dot(left, piece[0], preferred_element_type=jnp.float32)
    lower = jnp.dot(right, piece[1], preferred_element_type=jnp.float32)
    pre = (upper + lower).reshape(prompts_dev, npairs, width_local)
    hidden = jax.nn.gelu(pre + pref_bias)
    partial_logit = jnp.sum(hidden * pref_out, axis=-1)
    logit = lax.psum(partial_logit, "tensor")
    prob = jax.nn.sigmoid(logit)
    numbers = jnp.arange(groups, dtype=jnp.int32)
    first = (pairs[:, :, 0][:, :, None] == numbers).astype(jnp.float32)
    second = (pairs[:, :, 1][:, :, None] == numbers).astype(jnp.float32)
    wins = jnp.sum(prob[:, :, None] * first + (1.0 - prob)[:, :, None] * second, axis=1)
    count = jnp.sum(first + second, axis=1)
    winrate = (wins + 1.0) / (count + 2.0)
    placed = (owner[:, :, None] == numbers).astype(jnp.float32)
    rowrate = jnp.sum(winrate[:, :, None] * placed, axis=1).reshape(-1)
    coef = 2.0 * (logratio - eta_scale * (rowrate - 0.5))
    weighted = (
        (
            features.astype(jnp.float32).reshape(resp_dev, -1, features.shape[1])
            * coef[:, None, None]
        )
        .reshape(features.shape)
        .astype(jnp.bfloat16)
    )
    piece = lax.all_gather(w_out, "dp", axis=0, tiled=True)
    block = weighted
    d_attn = jnp.dot(block, piece, preferred_element_type=jnp.float32).astype(jnp.bfloat16)
    total_resp = resp_dev * lax.axis_size("dp")
    block = weighted
    o_grad = (
        lax.psum_scatter(
            lax.dot_general(
                block, attn_out, (((0,), (0,)), ((), ())), preferred_element_type=jnp.float32
            ),
            "dp",
            scatter_dimension=0,
            tiled=True,
        )
        / total_resp
    )
    return (d_attn, o_grad)


def solution(mesh):
    return jax.shard_map(
        shards,
        mesh=mesh,
        in_specs=(
            P("dp", None),
            P("dp", None),
            P("dp", None, None),
            P(None, "dp", "tensor"),
            P("tensor"),
            P("tensor"),
            P("dp"),
            P("dp", "tensor"),
            P("dp", "tensor"),
            P("dp", "tensor"),
        ),
        out_specs=(P("dp", "tensor"), P("dp", "tensor")),
        check_vma=False,
    )
```

profile of v0, /device:TPU:32, one launch (start us, length us, event | category | flops | bytes accessed | tf_op | source)
XLA Modules:
  0.0 641.9 jit_solution(11647005601567376183)
XLA Ops:
  7.2 0.0 copy-start
  7.2 0.0 copy-start.2
  7.2 0.0 all-gather.6.cloned.1.call-start
  7.2 0.7 all-gather.6.cloned.1.call-update
  7.9 0.0 all-gather.4.cloned.1.call-start
  8.0 0.7 all-gather.4.cloned.1.call-update
  8.7 0.0 all-gather.8.cloned.1.call-start
  8.7 0.7 all-gather.8.cloned.1.call-update
  9.4 0.0 reduce-scatter.2.cloned.1.call-start
  9.5 0.8 fusion.20
  10.2 0.1 reshape.143
  10.3 2.2 gather_fusion.2
  12.5 0.1 reshape.146
  12.6 0.1 reshape.148
  12.7 2.2 gather_fusion.3
  14.9 0.1 reshape.151
  15.0 0.1 fusion.16
  15.0 0.1 reshape.102
  15.1 0.1 reshape.101
  15.2 0.0 copy-done.2
  15.2 1.2 gather_fusion.1
  16.4 0.0 copy-start.3
  16.4 0.0 copy-start.4
  16.5 1.2 gather_fusion
  17.6 0.0 copy-start.1
  17.6 0.0 copy-start.5
  17.7 168.8 %all-gather.6.cloned.1.call-done = bf16[2,4608,576]{2,1,0:T(8,128)(2,1)} async-done(((bf16[2,144,576]{2,1,0:T(8,128)(2,1)}), bf16[2,4608,576]{2,1,0:T(8,128)(2,1)}) %all-gather.6.cloned.1.call-update) | async-done | bytes 10616848 | tf_op jit(solution)/shard_map/all_gather | solution.py:23
  186.5 3.8 fusion.2
  190.3 0.0 copy-done.3
  190.3 0.0 copy-done.4
  190.3 3.9 fusion.15
  194.2 0.1 reduce_sum.39
  194.3 15.1 %psum.7 = f32[2,56]{1,0:T(2,128)S(1)} all-reduce(f32[2,56]{1,0:T(2,128)S(1)} %reduce_sum.39), channel_id=1, replica_groups=mesh['dp'=32,'tensor'=8] {'tensor'}, use_global_device_ids=true, to_apply=%region_1.0 | all-reduce | flops 112 | bytes 896 | tf_op jit(solution)/shard_map/psum | solution.py:29
  209.4 0.1 add_reduce_fusion.1
  209.5 0.0 copy-done.1
  209.5 0.1 select_reduce_fusion
  209.6 0.1 mul.106
  209.7 0.0 copy-done.5
  209.7 0.1 mul.108
  209.8 0.1 mul.109
  209.8 75.3 %all-gather.4.cloned.1.call-done = bf16[1024,4608]{0,1:T(8,128)(2,1)} async-done(((bf16[1024,576]{0,1:T(8,128)(2,1)}), bf16[1024,4608]{0,1:T(8,128)(2,1)}) %all-gather.4.cloned.1.call-update) | async-done | bytes 9437200 | tf_op jit(solution)/shard_map/all_gather | solution.py:17
  285.1 0.0 copy-done
  285.1 11.2 %fusion = f32[4608,512]{1,0:T(8,128)} fusion(bf16[1024,512]{1,0:T(8,128)(2,1)S(1)} %copy-done, bf16[1024,4608]{0,1:T(8,128)(2,1)} %all-gather.4.cloned.1.call-done, f32[1024]{0:T(1024)S(1)} %mul.109), kind=kOutput, calls=%fused_computation.5 | convolution fusion | flops 4845993984 | bytes 19927040 | tf_op jit(solution)/shard_map/dot_general | solution.py:55
  296.4 0.0 reduce-scatter.2.cloned.1.call-update
  296.4 148.1 %all-gather.8.cloned.1.call-done = bf16[4608,512]{1,0:T(8,128)(2,1)} async-done(((bf16[144,512]{1,0:T(8,128)(2,1)}), bf16[4608,512]{1,0:T(8,128)(2,1)}) %all-gather.8.cloned.1.call-update) | async-done | bytes 4718608 | tf_op jit(solution)/shard_map/all_gather | solution.py:48
  444.5 9.8 %fusion.4 = bf16[1024,512]{1,0:T(8,128)(2,1)} fusion(bf16[4608,512]{1,0:T(8,128)(2,1)} %all-gather.8.cloned.1.call-done, bf16[1024,4608]{0,1:T(8,128)(2,1)} %all-gather.4.cloned.1.call-done, f32[1024]{0:T(1024)S(1)} %mul.109), kind=kOutput, calls=%fused_computation.11 | convolution fusion | flops 4846518272 | bytes 15208448 | tf_op jit(solution)/shard_map/dot_general | solution.py:50
  454.3 179.3 %reduce-scatter.2.cloned.1.call-done = f32[144,512]{1,0:T(8,128)} async-done(((f32[4608,512]{1,0:T(8,128)}), f32[144,512]{1,0:T(8,128)}) %reduce-scatter.2.cloned.1.call-update) | async-done | bytes 294928 | tf_op jit(solution)/shard_map/reduce_scatter | solution.py:54
  633.6 1.7 broadcast_multiply_fusion
  (11 shorter events, 0.1 us)
Async XLA Ops:
  7.2 278.0 %copy-start = (bf16[1024,512]{1,0:T(8,128)(2,1)S(1)}, bf16[1024,512]{1,0:T(8,128)(2,1)}, u32[]{:S(2)}) copy-start(bf16[1024,512]{1,0:T(8,128)(2,1)} %param.19) | copy-start | bytes 3145732
  7.2 8.0 %copy-start.2 = (bf16[16,4608]{1,0:T(8,128)(2,1)S(1)}, bf16[16,4608]{1,0:T(8,128)(2,1)}, u32[]{:S(2)}) copy-start(bf16[16,4608]{1,0:T(8,128)(2,1)} %param.12) | copy-start | bytes 442372
  7.2 179.3 %all-gather.6.cloned.1.call-start = ((), (), s32[]{:S(2)}) async-start(), calls=%async_computation.2 | async-start | bytes 12165120 | tf_op jit(solution)/shard_map/all_gather | solution.py:23
  7.9 277.2 %all-gather.4.cloned.1.call-start = ((), (), s32[]{:S(2)}) async-start(), calls=%async_computation.1 | async-start | bytes 10616832 | tf_op jit(solution)/shard_map/all_gather | solution.py:17
  8.7 435.8 %all-gather.8.cloned.1.call-start = ((), (), s32[]{:S(2)}) async-start(), calls=%async_computation.3 | async-start | bytes 4866048 | tf_op jit(solution)/shard_map/all_gather | solution.py:48
  9.4 624.2 %reduce-scatter.2.cloned.1.call-start = ((), (), s32[]{:S(2)}) async-start(), calls=%async_computation.4 | async-start | bytes 9732096 | tf_op jit(solution)/shard_map/reduce_scatter | solution.py:54
  16.4 173.9 %copy-start.3 = (f32[576]{0:T(1024)S(1)}, f32[576]{0:T(1024)}, u32[]{:S(2)}) copy-start(f32[576]{0:T(1024)} %param.17) | copy-start | bytes 6916
  16.4 173.9 %copy-start.4 = (f32[576]{0:T(1024)S(1)}, f32[576]{0:T(1024)}, u32[]{:S(2)}) copy-start(f32[576]{0:T(1024)} %param.16) | copy-start | bytes 6916
  17.6 191.9 %copy-start.1 = (s32[2,8]{1,0:T(2,128)S(1)}, s32[2,8]{1,0:T(2,128)}, u32[]{:S(2)}) copy-start(s32[2,8]{1,0:T(2,128)} %param.13) | copy-start | bytes 196
  17.6 192.0 %copy-start.5 = (f32[16]{0:T(128)S(1)}, f32[16]{0:T(128)}, u32[]{:S(2)}) copy-start(f32[16]{0:T(128)} %param.18) | copy-start | bytes 196
Sparse Core Ops, SparseCore 0:
  9.8 176.6 all-gather.5
  188.3 96.7 all-gather.3
  286.9 157.4 all-gather.7
  446.9 186.7 reduce-scatter.1
where the time goes:
time: 642 us
  waiting for transfers between devices  574 us (89%)
  matrix products  28.8 us (4%)
  blocking collectives  15.1 us (2%)
  between operations  13.9 us (2%)
  local copies, waits for them, and re-layouts  8.34 us (1%)
    reduce_scatter x1, waiting for transfers between devices, shards(): lax.psum_scatter(lax.dot_general(block, attn_out, (((0,), (0,)), ((), ())...  179 us
    all_gather x1, waiting for transfers between devices, shards(): piece = lax.all_gather(pref_weight, 'dp', axis=1, tiled=True)  169 us
    all_gather x1, waiting for transfers between devices, shards(): piece = lax.all_gather(w_out, 'dp', axis=0, tiled=True)  148 us
    all_gather x1, waiting for transfers between devices, shards(): features = lax.all_gather(grad_out, 'tensor', axis=1, tiled=True)  75.3 us
    psum x1, blocking collectives, shards(): logit = lax.psum(partial_logit, 'tensor')  15.1 us
  transfers between devices with their start and end apart: 4, of which 4 were waited for; matrix products, arithmetic and copies ran while one was open for 6% of the time, Pallas kernels for 0%

commit v1 on v0

--- a/solution.py
+++ b/solution.py
@@ -14,7 +14,9 @@
     groups = owner.shape[1]
     npairs = pairs.shape[1]
     width_local = pref_weight.shape[2]
-    features = lax.all_gather(grad_out, "tensor", axis=1, tiled=True)
+    features = jnp.concatenate(
+        lax.all_to_all(jnp.stack([grad_out] * lax.axis_size("tensor")), "tensor", 0, 0), axis=1
+    )
     base = (jnp.arange(prompts_dev, dtype=jnp.int32) * groups)[:, None]
     row_a = base + jnp.take_along_axis(owner, pairs[:, :, 0], axis=1)
     row_b = base + jnp.take_along_axis(owner, pairs[:, :, 1], axis=1)

time: 642 us -> 719 us (1.12)
  waiting for transfers between devices: 574 us -> 627 us
  other arithmetic: 2.02 us -> 12.2 us
  starting transfers between devices: 0.15 us -> 7.81 us
    all_gather x1, waiting for transfers between devices: 169 us -> 330 us  [shards(): piece = lax.all_gather(pref_weight, 'dp', axis=1, tiled=True)]
    all_gather x1 -> x0, waiting for transfers between devices: 75.3 us -> none  [shards(): features = lax.all_gather(grad_out, 'tensor', axis=1, tiled=True)]
    all_gather x1, waiting for transfers between devices: 148 us -> 115 us  [shards(): piece = lax.all_gather(w_out, 'dp', axis=0, tiled=True)]
    convert_element_type x0 -> x1, other arithmetic: none -> 10.2 us  [shards(): weighted = (features.astype(jnp.float32).reshape(resp_dev, -1, features.s...]
    all_to_all x0 -> x1, starting transfers between devices: none -> 7.7 us  [shards(): lax.all_to_all(jnp.stack([grad_out] * lax.axis_size('tensor')), 'tensor',...]
  transfers between devices with their start and end apart: 4 -> 4, of which waited for: 4 -> 3; matrix products, arithmetic and copies ran while one was open for 6% -> 7% of each run, Pallas kernels for 0% -> 0%
where the time goes in v1:
time: 719 us; the launch traced here: 718 us
  waiting for transfers between devices  627 us (87%)
  matrix products  28.8 us (4%)
  blocking collectives  15.4 us (2%)
  between operations  13.9 us (2%)
  local copies, waits for them, and re-layouts  13.4 us (2%)
  other arithmetic  12.2 us (2%)
  starting transfers between devices  7.81 us (1%)
    all_gather x1, waiting for transfers between devices, shards(): piece = lax.all_gather(pref_weight, 'dp', axis=1, tiled=True)  330 us
    reduce_scatter x1, waiting for transfers between devices, shards(): lax.psum_scatter(lax.dot_general(block, attn_out, (((0,), (0,)), ((), ())...  180 us
    all_gather x1, waiting for transfers between devices, shards(): piece = lax.all_gather(w_out, 'dp', axis=0, tiled=True)  115 us
    psum x1, blocking collectives, shards(): logit = lax.psum(partial_logit, 'tensor')  15.4 us
  transfers between devices with their start and end apart: 4, of which 3 were waited for; matrix products, arithmetic and copies ran while one was open for 7% of the time, Pallas kernels for 0%

profile of v1, /device:TPU:32, one launch (start us, length us, event | category | flops | bytes accessed | tf_op | source)
XLA Modules:
  0.0 718.3 jit_solution(8513090795073435907)
XLA Ops:
  7.2 0.0 copy-start
  7.2 0.0 all-gather.3.cloned.1.call-start
  7.2 0.7 all-gather.3.cloned.1.call-update
  7.9 6.2 stack.2
  14.1 0.0 copy-start.3
  14.1 0.0 copy-start.1
  14.1 0.0 copy-start.2
  14.1 7.7 %all-to-all-start = ((bf16[8,1024,576]{1,2,0:T(8,128)(2,1)}), bf16[8,1024,576]{1,2,0:T(8,128)(2,1)}, u32[]{:S(2)}, u32[]{:S(2)}) async-start(bf16[8,1024,576]{1,2,0:T(8,128)(2,1)} %stack.2), calls=%async_computation | async-start | bytes 18874368 | tf_op jit(solution)/shard_map/all_to_all | solution.py:18
  21.8 0.0 all-gather.5.cloned.1.call-start
  21.8 0.7 all-gather.5.cloned.1.call-update
  22.5 0.0 reduce-scatter.2.cloned.1.call-start
  22.6 0.0 copy-done.3
  22.6 0.1 reshape.152
  22.7 0.0 copy-done.1
  22.7 2.0 gather_fusion.2
  24.7 0.1 reshape.155
  24.8 0.1 reshape.157
  24.9 2.0 gather_fusion.3
  26.9 0.1 reshape.160
  27.0 0.1 fusion.14
  27.1 0.1 reshape.110
  27.2 0.1 reshape.109
  27.3 0.0 copy-done.2
  27.3 1.2 gather_fusion.1
  28.4 0.0 copy-start.4
  28.5 0.0 copy-start.5
  28.5 1.2 gather_fusion
  29.7 0.0 copy-start.6
  29.7 330.4 %all-gather.3.cloned.1.call-done = bf16[2,4608,576]{2,1,0:T(8,128)(2,1)} async-done(((bf16[2,144,576]{2,1,0:T(8,128)(2,1)}), bf16[2,4608,576]{2,1,0:T(8,128)(2,1)}) %all-gather.3.cloned.1.call-update) | async-done | bytes 10616848 | tf_op jit(solution)/shard_map/all_gather | solution.py:25
  360.1 3.8 fusion.1
  363.9 0.0 copy-done.4
  363.9 0.0 copy-done.5
  363.9 4.0 fusion.13
  367.9 0.1 reduce_sum.39
  368.0 15.4 %psum.7 = f32[2,56]{1,0:T(2,128)S(1)} all-reduce(f32[2,56]{1,0:T(2,128)S(1)} %reduce_sum.39), channel_id=1, replica_groups=mesh['dp'=32,'tensor'=8] {'tensor'}, use_global_device_ids=true, to_apply=%region_1.0 | all-reduce | flops 112 | bytes 896 | tf_op jit(solution)/shard_map/psum | solution.py:31
  383.4 0.1 add_reduce_fusion.1
  383.5 0.1 select_reduce_fusion
  383.6 0.1 mul.106
  383.7 0.0 copy-done.6
  383.7 0.1 mul.108
  383.8 0.1 mul.109
  383.9 0.0 all-to-all-done
  383.9 10.2 %fusion = bf16[1024,4608]{0,1:T(8,128)(2,1)} fusion(f32[1024]{0:T(1024)S(1)} %mul.109, bf16[8,1024,576]{1,2,0:T(8,128)(2,1)} %all-to-all-done), kind=kLoop, calls=%fused_computation.5 | loop fusion | flops 14155776 | bytes 18878464 | tf_op jit(solution)/shard_map/convert_element_type | solution.py:48
  394.1 0.0 copy-done
  394.1 11.2 %fusion.19 = f32[4608,512]{1,0:T(8,128)} fusion(bf16[1024,4608]{0,1:T(8,128)(2,1)} %fusion, bf16[1024,512]{1,0:T(8,128)(2,1)S(1)} %copy-done), kind=kOutput, calls=%fused_computation.52 | convolution fusion | flops 4831838208 | bytes 19922944 | tf_op jit(solution)/shard_map/dot_general | solution.py:57
  405.2 0.0 reduce-scatter.2.cloned.1.call-update
  405.3 115.1 %all-gather.5.cloned.1.call-done = bf16[4608,512]{1,0:T(8,128)(2,1)} async-done(((bf16[144,512]{1,0:T(8,128)(2,1)}), bf16[4608,512]{1,0:T(8,128)(2,1)}) %all-gather.5.cloned.1.call-update) | async-done | bytes 4718608 | tf_op jit(solution)/shard_map/all_gather | solution.py:50
  520.4 9.8 %convolution_convert_fusion = bf16[1024,512]{1,0:T(8,128)(2,1)} fusion(bf16[1024,4608]{0,1:T(8,128)(2,1)} %fusion, bf16[4608,512]{1,0:T(8,128)(2,1)} %all-gather.5.cloned.1.call-done), kind=kOutput, calls=%fused_computation.10 | convolution fusion | flops 4832362496 | bytes 15204352 | tf_op jit(solution)/shard_map/dot_general | solution.py:52
  530.2 179.9 %reduce-scatter.2.cloned.1.call-done = f32[144,512]{1,0:T(8,128)} async-done(((f32[4608,512]{1,0:T(8,128)}), f32[144,512]{1,0:T(8,128)}) %reduce-scatter.2.cloned.1.call-update) | async-done | bytes 294928 | tf_op jit(solution)/shard_map/reduce_scatter | solution.py:56
  710.1 1.7 broadcast_multiply_fusion
  (12 shorter events, 0.1 us)
Async XLA Ops:
  7.2 386.9 %copy-start = (bf16[1024,512]{1,0:T(8,128)(2,1)S(1)}, bf16[1024,512]{1,0:T(8,128)(2,1)}, u32[]{:S(2)}) copy-start(bf16[1024,512]{1,0:T(8,128)(2,1)} %param.19) | copy-start | bytes 3145732
  7.2 352.9 %all-gather.3.cloned.1.call-start = ((), (), s32[]{:S(2)}) async-start(), calls=%async_computation.2 | async-start | bytes 12165120 | tf_op jit(solution)/shard_map/all_gather | solution.py:25
  14.1 8.5 %copy-start.3 = (s32[2,56,2]{1,2,0:T(2,128)S(1)}, s32[2,56,2]{1,2,0:T(2,128)}, u32[]{:S(2)}) copy-start(s32[2,56,2]{1,2,0:T(2,128)} %param.14) | copy-start | bytes 2692
  14.1 8.6 %copy-start.1 = (s32[2,8]{1,0:T(2,128)S(1)}, s32[2,8]{1,0:T(2,128)}, u32[]{:S(2)}) copy-start(s32[2,8]{1,0:T(2,128)} %param.13) | copy-start | bytes 196
  14.1 13.2 %copy-start.2 = (bf16[16,4608]{1,0:T(8,128)(2,1)S(1)}, bf16[16,4608]{1,0:T(8,128)(2,1)}, u32[]{:S(2)}) copy-start(bf16[16,4608]{1,0:T(8,128)(2,1)} %param.12) | copy-start | bytes 442372
  14.1 369.8 %all-to-all-start = ((bf16[8,1024,576]{1,2,0:T(8,128)(2,1)}), bf16[8,1024,576]{1,2,0:T(8,128)(2,1)}, u32[]{:S(2)}, u32[]{:S(2)}) async-start(bf16[8,1024,576]{1,2,0:T(8,128)(2,1)} %stack.2), calls=%async_computation | async-start | bytes 18874368 | tf_op jit(solution)/shard_map/all_to_all | solution.py:18
  21.8 498.6 %all-gather.5.cloned.1.call-start = ((), (), s32[]{:S(2)}) async-start(), calls=%async_computation.3 | async-start | bytes 4866048 | tf_op jit(solution)/shard_map/all_gather | solution.py:50
  22.5 687.6 %reduce-scatter.2.cloned.1.call-start = ((), (), s32[]{:S(2)}) async-start(), calls=%async_computation.4 | async-start | bytes 9732096 | tf_op jit(solution)/shard_map/reduce_scatter | solution.py:56
  28.4 335.5 %copy-start.4 = (f32[576]{0:T(1024)S(1)}, f32[576]{0:T(1024)}, u32[]{:S(2)}) copy-start(f32[576]{0:T(1024)} %param.17) | copy-start | bytes 6916
  28.5 335.5 %copy-start.5 = (f32[576]{0:T(1024)S(1)}, f32[576]{0:T(1024)}, u32[]{:S(2)}) copy-start(f32[576]{0:T(1024)} %param.16) | copy-start | bytes 6916
  29.7 354.1 %copy-start.6 = (f32[16]{0:T(128)S(1)}, f32[16]{0:T(128)}, u32[]{:S(2)}) copy-start(f32[16]{0:T(128)} %param.18) | copy-start | bytes 196
Sparse Core Ops, SparseCore 0:
  9.8 350.2 all-gather.2
  361.8 158.5 all-gather.4
  523.0 187.0 reduce-scatter.1
